TPU v7x, 256 devices: a whole 4x4x8 slice. The times are simulated.
256 devices in a mesh: seq: 64 (over y, z, core), head: 4 (over x).
Axes of the slice: x: 4, y: 4, z: 8, core: 2. Of those that a mesh axis runs over, the one named last changes fastest.
Arguments:
- queries: bfloat16 [8192, 1024], P('seq', 'head'), may hold values from -6 to 6
- raw_keys: bfloat16 [8192, 1024], P('seq', 'head'), may hold values from -6 to 6
- values: bfloat16 [8192, 1024], P('seq', 'head'), may hold values from -6 to 6
- write_rate: float32 [8192, 8], P('seq', 'head'), may hold values from 0.0005 to 1
- out_weight: bfloat16 [1024, 1024], P('head'), may hold values from -0.1875 to 0.1875
- out_grad: bfloat16 [8192, 1024], P('seq', 'head'), may hold values from -6 to 6
Outputs:
- layer_out: bfloat16 [8192, 1024], P('seq', 'head')
- query_grad: bfloat16 [8192, 1024], P('seq', 'head')
- key_grad: bfloat16 [8192, 1024], P('seq', 'head')
- value_grad: bfloat16 [8192, 1024], P('seq', 'head')
- rate_grad: float32 [8192, 8], P('seq', 'head')
All inputs are finite; a program needn't handle non-finite values.
Results may differ from a plain program's by a relative error of at most 0.0049.
Values may be sent and summed in bfloat16 or wider, within the bound.
No kernel may reach another device: no remote copies, remote signals or barrier semaphores. Data moves between devices by JAX's collectives and lax.ppermute only.
A program may use at most 128 MiB of HBM per device.

v0:
```python
import jax
import jax.numpy as jnp
from jax import lax
from jax.sharding import PartitionSpec as P

BLOCK = 64
epsilon = 1e-06
highest = lax.Precision.HIGHEST


def prefix(part, axis, combine, identity, reverse):
    count = lax.axis_size(axis)
    place = lax.axis_index(axis)
    ahead = count - 1 - place if reverse else place
    gathered = jax.tree.map(lambda a: lax.all_gather(a, axis), part)
    state = jax.tree.map(lambda a, e: jnp.zeros_like(a) + jnp.asarray(e, a.dtype), part, identity)

    def one(turn, state):
        source = count - 1 - turn if reverse else turn
        return combine(
            state, jax.tree.map(lambda a: lax.dynamic_index_in_dim(a, source, 0, False), gathered)
        )

    return lax.fori_loop(0, ahead, one, state)


def unit_rows(array):
    return array * lax.rsqrt(jnp.sum(array * array, -1, keepdims=True) + epsilon)


def to_blocks(array, head_count):
    rows = array.shape[0]
    head_width = array.shape[1] // head_count
    return array.reshape(rows // BLOCK, BLOCK, head_count, head_width).transpose(2, 0, 1, 3)


def rate_blocks(decay_rate):
    rows = decay_rate.shape[0]
    head_count = decay_rate.shape[1]
    return decay_rate.reshape(rows // BLOCK, BLOCK, head_count).transpose(2, 0, 1)


def from_blocks(block_outputs):
    block_count, head_count, size, head_width = block_outputs.shape
    return block_outputs.transpose(0, 2, 1, 3).reshape(block_count * size, head_count * head_width)


def block_factors(query_blocks, key_blocks, value_blocks, rate_parts):
    unit_query = unit_rows(query_blocks)
    unit_key = unit_rows(key_blocks)
    size = unit_key.shape[-2]
    identity_block = jnp.eye(size, dtype=jnp.float32)
    key_gram = jnp.einsum(
        "hncd,hnsd->hncs", unit_key * rate_parts[..., None], unit_key, precision=highest
    )
    strict_lower = jnp.tril(key_gram, -1)
    result = identity_block - strict_lower
    power_term = strict_lower
    span_done = 2
    while span_done < size:
        power_term = jnp.einsum("hnij,hnjk->hnik", power_term, power_term, precision=highest)
        result = result + jnp.einsum("hnij,hnjk->hnik", result, power_term, precision=highest)
        span_done = span_done * 2
    scaled = result * rate_parts[..., None, :]
    key_mix = jnp.einsum("hncs,hnsd->hncd", scaled, unit_key, precision=highest)
    value_mix = jnp.einsum("hncs,hnsd->hncd", scaled, value_blocks, precision=highest)
    causal_scores = jnp.tril(jnp.einsum("hncd,hnsd->hncs", unit_query, unit_key, precision=highest))
    return (unit_query, unit_key, key_mix, value_mix, causal_scores)


def run_blocks(factors, start_state):
    moved = tuple((jnp.moveaxis(member, 1, 0) for member in factors))

    def advance_block(state, pieces):
        unit_query, unit_key, key_mix, value_mix, causal_scores = pieces
        innovation = value_mix - jnp.einsum("hcd,hde->hce", key_mix, state, precision=highest)
        block_out = jnp.einsum("hcd,hde->hce", unit_query, state, precision=highest)
        block_out = block_out + jnp.einsum(
            "hcs,hse->hce", causal_scores, innovation, precision=highest
        )
        state = state + jnp.einsum("hcd,hce->hde", unit_key, innovation, precision=highest)
        return (state, block_out)

    return lax.scan(advance_block, start_state, moved)


def compose(earlier, later):
    early_map, early_shift = earlier
    late_map, late_shift = later
    joined_map = jnp.einsum("hij,hjk->hik", late_map, early_map, precision=highest)
    joined_shift = jnp.einsum("hij,hjk->hik", late_map, early_shift, precision=highest) + late_shift
    return (joined_map, joined_shift)


def body(queries, raw_keys, values, write_rate, out_weight, out_grad):
    head_count = write_rate.shape[1]
    head_width = queries.shape[1] // head_count
    token_count = queries.shape[0]

    def factor_inputs(float_query, float_key, float_value, rates):
        return block_factors(
            to_blocks(float_query, head_count),
            to_blocks(float_key, head_count),
            to_blocks(float_value, head_count),
            rate_blocks(rates),
        )

    factors, pull_factors = jax.vjp(
        factor_inputs,
        queries.astype(jnp.float32),
        raw_keys.astype(jnp.float32),
        values.astype(jnp.float32),
        write_rate,
    )
    unit_query, unit_key, key_mix, value_mix, causal_scores = factors
    identity_heads = jnp.broadcast_to(
        jnp.eye(head_width, dtype=jnp.float32), (head_count, head_width, head_width)
    )
    zero_heads = jnp.zeros((head_count, head_width, head_width), jnp.float32)
    widened = (
        unit_query,
        unit_key,
        key_mix,
        jnp.concatenate([jnp.zeros_like(value_mix), value_mix], -1),
        causal_scores,
    )
    joined_state, joined_outputs = run_blocks(
        widened, jnp.concatenate([identity_heads, zero_heads], -1)
    )
    transition = joined_state[..., :head_width]
    offset = joined_state[..., head_width:]
    query_effect = joined_outputs[..., :head_width]
    attended_grad = lax.dot_general(
        lax.all_gather(out_grad, "head", axis=1, tiled=True),
        out_weight,
        (((1,), (1,)), ((), ())),
        preferred_element_type=jnp.float32,
    )
    grad_blocks = attended_grad.reshape(
        token_count // BLOCK, BLOCK, head_count, head_width
    ).transpose(0, 2, 1, 3)
    local_adjoint = jnp.einsum("nhcd,nhce->hde", query_effect, grad_blocks, precision=highest)
    unused_map, entry_state = prefix(
        (transition, offset), "seq", compose, (identity_heads, zero_heads), False
    )
    unused_adjoint_map, exit_adjoint = prefix(
        (jnp.swapaxes(transition, 1, 2), local_adjoint),
        "seq",
        compose,
        (identity_heads, zero_heads),
        True,
    )

    def run_from_entry(factor_tuple):
        return run_blocks(factor_tuple, entry_state)

    (final_state, block_outputs), pull_run = jax.vjp(run_from_entry, factors)
    factor_grads = pull_run((exit_adjoint, grad_blocks))
    query_part, key_part, value_part, rate_grad = pull_factors(factor_grads[0])
    attended_bf = from_blocks(block_outputs).astype(jnp.bfloat16)
    partial_out = jnp.dot(attended_bf, out_weight, preferred_element_type=jnp.float32)
    layer_out = lax.psum_scatter(partial_out, "head", scatter_dimension=1, tiled=True).astype(
        jnp.bfloat16
    )
    return (
        layer_out,
        query_part.astype(jnp.bfloat16),
        key_part.astype(jnp.bfloat16),
        value_part.astype(jnp.bfloat16),
        rate_grad,
    )


def solution(mesh):
    placed = (
        P("seq", "head"),
        P("seq", "head"),
        P("seq", "head"),
        P("seq", "head"),
        P("head", None),
        P("seq", "head"),
    )
    return jax.shard_map(
        body,
        mesh=mesh,
        in_specs=placed,
        out_specs=(
            P("seq", "head"),
            P("seq", "head"),
            P("seq", "head"),
            P("seq", "head"),
            P("seq", "head"),
        ),
        check_vma=False,
    )
```

profile of v0, /device:TPU:8, one launch (start us, length us, event | category | flops | bytes accessed | tf_op | source)
XLA Modules:
  0.0 506.4 jit_solution(13383869806528043871)
XLA Ops:
  16.5 4.0 while.78
  20.5 12.6 %all_gather.33 = bf16[128,1024]{1,0:T(8,128)(2,1)S(1)} all-gather(bf16[128,256]{1,0:T(8,128)(2,1)S(1)} %copy-done.15), channel_id=1, replica_groups=mesh['seq'=64,'head'=4] {'head'}, dimensions={1}, use_global_device_ids=true | all-gather | bytes 327680 | tf_op jit(solution)/shard_map/all_gather | solution.py:134
  33.5 1.9 convolution_bitcast_fusion.4
  39.1 80.6 %all-gather.15.cloned.1.call-done = f32[128,128,128]{2,1,0:T(8,128)} async-done(((f32[2,128,128]{2,1,0:T(8,128)}), f32[128,128,128]{2,1,0:T(8,128)}) %all-gather.15.cloned.1.call-update) | async-done | bytes 8388624 | tf_op jit(solution)/shard_map/all_gather | solution.py:15
  119.6 82.6 %all-gather.13.cloned.1.call-done = f32[128,128,128]{2,1,0:T(8,128)} async-done(((f32[2,128,128]{2,1,0:T(8,128)}), f32[128,128,128]{2,1,0:T(8,128)}) %all-gather.13.cloned.1.call-update) | async-done | bytes 8388624 | tf_op jit(solution)/shard_map/all_gather | solution.py:15
  202.2 60.8 %while.81 = (s32[]{:T(128)}, f32[2,128,128]{2,1,0:T(8,128)S(1)}, s32[]{:T(128)}, f32[64,2,128,128]{3,2,1,0:T(8,128)}, f32[64,2,128,128]{3,2,1,0:T(8,128)}, /*index=5*/s32[]{:T(128)}, s32[]{:T(128)}, s32[]{:T(128)}, s32[]{:T(128)}) while((s32[]{:T(128)}, f32[2,128,128]{2,1,0:T(8,128)S(1)}, s32[]{:T(128)}, f32[64,2,128,128]{3,2,1,0:T(8,128)}, ...), condition=%wide.region_10.11_spmd, body=%wide.region_9.10_spmd.sunk | while | flops 50364420 | bytes 787595 | solution.py:24
  213.9 1.2 convolution_add_fusion.38
  215.2 1.3 convolution_add_fusion.38
  219.1 1.2 convolution_add_fusion.38
  221.7 1.2 convolution_add_fusion.38
  225.6 1.2 convolution_add_fusion.38
  228.1 1.2 convolution_add_fusion.38
  229.4 1.2 convolution_add_fusion.38
  241.1 1.2 convolution_add_fusion.38
  252.7 1.2 convolution_add_fusion.38
  257.9 1.3 convolution_add_fusion.38
  259.2 1.3 convolution_add_fusion.38
  263.1 21.8 %all-gather.9.cloned.1.call-done = f32[128,128,128]{2,1,0:T(8,128)} async-done(((f32[2,128,128]{2,1,0:T(8,128)}), f32[128,128,128]{2,1,0:T(8,128)}) %all-gather.9.cloned.1.call-update) | async-done | bytes 8388624 | tf_op jit(solution)/shard_map/all_gather | solution.py:15
  284.9 82.4 %all-gather.11.cloned.1.call-done = f32[128,128,128]{2,1,0:T(8,128)} async-done(((f32[2,128,128]{2,1,0:T(8,128)}), f32[128,128,128]{2,1,0:T(8,128)}) %all-gather.11.cloned.1.call-update) | async-done | bytes 8388624 | tf_op jit(solution)/shard_map/all_gather | solution.py:15
  367.3 20.8 %while.79 = (s32[]{:T(128)}, f32[2,128,128]{2,1,0:T(8,128)S(1)}, s32[]{:T(128)}, f32[64,2,128,128]{3,2,1,0:T(8,128)}, f32[64,2,128,128]{3,2,1,0:T(8,128)}, /*index=5*/s32[]{:T(128)}, s32[]{:T(128)}, s32[]{:T(128)}) while((s32[]{:T(128)}, f32[2,128,128]{2,1,0:T(8,128)S(1)}, s32[]{:T(128)}, f32[64,2,128,128]{3,2,1,0:T(8,128)}, ...), condition=%wide.region_5.6_spmd, body=%wide.region_4.5_spmd.sunk | while | flops 50364420 | bytes 787575 | solution.py:24
  388.2 3.5 while.80
  394.3 10.4 %while.82 = (s32[]{:T(128)}, f32[2,128,128]{2,1,0:T(8,128)S(1)}, f32[2,2,64,128]{3,2,0,1:T(8,128)}, f32[2,2,64,128]{3,2,0,1:T(8,128)}, f32[2,2,64,128]{3,2,1,0:T...) while((s32[]{:T(128)}, f32[2,128,128]{2,1,0:T(8,128)S(1)}, ...), condition=%wide.region_12.13_spmd, body=%wide.region_11.12_spmd.sunk | while | flops 176275456 | bytes 2367137 | solution.py:84
  420.9 77.4 %reduce-scatter.2.cloned.1.call-done = f32[128,256]{1,0:T(8,128)} async-done(((f32[128,1024]{1,0:T(8,128)}), f32[128,256]{1,0:T(8,128)}) %reduce-scatter.2.cloned.1.call-update) | async-done | bytes 131088 | tf_op jit(solution)/shard_map/reduce_scatter | solution.py:162
  498.3 1.5 convert_element_type.51
  (298 shorter events, 114.2 us)
Async XLA Ops:
  7.2 25.9 %copy-start = (bf16[256,1024]{1,0:T(8,128)(2,1)S(1)}, bf16[256,1024]{1,0:T(8,128)(2,1)}, u32[]{:S(2)}) copy-start(bf16[256,1024]{1,0:T(8,128)(2,1)} %param.20) | copy-start | bytes 1572868
  7.2 112.4 %all-gather.15.cloned.1.call-start = ((), (), s32[]{:S(2)}) async-start(), calls=%async_computation.5 | async-start | bytes 8519680 | tf_op jit(solution)/shard_map/all_gather | solution.py:15
  7.2 4.0 copy-start.10
  8.4 3.7 copy-start.20
  9.4 2.7 copy-start.18
  10.3 4.7 copy-start.16
  12.4 8.1 %copy-start.15 = (bf16[128,256]{1,0:T(8,128)(2,1)S(1)}, bf16[128,256]{1,0:T(8,128)(2,1)}, u32[]{:S(2)}) copy-start(bf16[128,256]{1,0:T(8,128)(2,1)} %param.21) | copy-start | bytes 196612
  12.7 3.8 copy-start.1
  35.4 166.8 %all-gather.13.cloned.1.call-start = ((), (), s32[]{:S(2)}) async-start(), calls=%async_computation.4 | async-start | bytes 8519680 | tf_op jit(solution)/shard_map/all_gather | solution.py:15
  37.0 247.8 %all-gather.9.cloned.1.call-start = ((), (), s32[]{:S(2)}) async-start(), calls=%async_computation.2 | async-start | bytes 8519680 | tf_op jit(solution)/shard_map/all_gather | solution.py:15
  37.8 329.5 %all-gather.11.cloned.1.call-start = ((), (), s32[]{:S(2)}) async-start(), calls=%async_computation.3 | async-start | bytes 8519680 | tf_op jit(solution)/shard_map/all_gather | solution.py:15
  38.3 460.0 %reduce-scatter.2.cloned.1.call-start = ((), (), s32[]{:S(2)}) async-start(), calls=%async_computation.1 | async-start | bytes 655360 | tf_op jit(solution)/shard_map/reduce_scatter | solution.py:162
  392.4 17.0 %copy-start.2 = (f32[2,2,64,64]{3,2,1,0:T(8,128)S(1)}, f32[2,2,64,64]{3,2,1,0:T(8,128)}, u32[]{:S(2)}) copy-start(f32[2,2,64,64]{3,2,1,0:T(8,128)} %copy-done.1) | copy-start | bytes 196612
  394.3 17.3 %copy-start.4 = (f32[2,2,64,64]{3,2,1,0:T(8,128)S(1)}, f32[2,2,64,64]{3,2,1,0:T(8,128)}, u32[]{:S(2)}) copy-start(f32[2,2,64,64]{3,2,1,0:T(8,128)} %copy-done.3) | copy-start | bytes 196612
  404.7 8.1 %copy-start.11 = (f32[64,64]{1,0:T(8,128)S(1)}, f32[64,64]{1,0:T(8,128)}, u32[]{:S(2)}) copy-start(f32[64,64]{1,0:T(8,128)} %copy-done.10) | copy-start | bytes 49156
  404.7 9.2 %copy-start.14 = (pred[64,64]{1,0:T(8,128)(4,1)S(1)}, pred[64,64]{1,0:T(8,128)(4,1)}, u32[]{:S(2)}) copy-start(pred[64,64]{1,0:T(8,128)(4,1)} %copy-done.13) | copy-start | bytes 12292
  404.7 10.0 %copy-start.7 = (f32[2,2,64,64]{3,2,1,0:T(8,128)S(1)}, f32[2,2,64,64]{3,2,1,0:T(8,128)}, u32[]{:S(2)}) copy-start(f32[2,2,64,64]{3,2,1,0:T(8,128)} %get-tuple-element.516) | copy-start | bytes 196612
  404.7 10.0 %copy-start.17 = (f32[2,2,64]{2,1,0:T(2,128)S(1)}, f32[2,2,64]{2,1,0:T(2,128)}, u32[]{:S(2)}) copy-start(f32[2,2,64]{2,1,0:T(2,128)} %copy-done.16) | copy-start | bytes 3076
  404.7 10.5 %copy-start.6 = (f32[2,2,64,128]{3,2,0,1:T(8,128)S(1)}, f32[2,2,64,128]{3,2,0,1:T(8,128)}, u32[]{:S(2)}) copy-start(f32[2,2,64,128]{3,2,0,1:T(8,128)} %get-tuple-element.517) | copy-start | bytes 393220
  404.8 11.0 %copy-start.21 = (f32[2,2,64]{2,1,0:T(2,128)S(1)}, f32[2,2,64]{2,1,0:T(2,128)}, u32[]{:S(2)}) copy-start(f32[2,2,64]{2,1,0:T(2,128)} %copy-done.20) | copy-start | bytes 3076
  404.8 11.0 %copy-start.12 = (bf16[2,2,64,128]{3,2,1,0:T(8,128)(2,1)S(1)}, bf16[2,2,64,128]{3,2,1,0:T(8,128)(2,1)}, u32[]{:S(2)}) copy-start(bf16[2,2,64,128]{3,2,1,0:T(8,128)(2,1)} %get-tuple-element.510) | copy-start | bytes 196612
  404.8 13.7 %copy-start.8 = (f32[2,2,64,128]{3,2,1,0:T(8,128)S(1)}, f32[2,2,64,128]{3,2,1,0:T(8,128)}, u32[]{:S(2)}) copy-start(f32[2,2,64,128]{3,2,1,0:T(8,128)} %get-tuple-element.519) | copy-start | bytes 393220
  404.8 14.8 %copy-start.5 = (f32[2,2,64,128]{3,2,0,1:T(8,128)S(1)}, f32[2,2,64,128]{3,2,0,1:T(8,128)}, u32[]{:S(2)}) copy-start(f32[2,2,64,128]{3,2,0,1:T(8,128)} %get-tuple-element.515) | copy-start | bytes 393220
  404.8 15.3 %copy-start.19 = (f32[2,2,64]{2,1,0:T(2,128)S(1)}, f32[2,2,64]{2,1,0:T(2,128)}, u32[]{:S(2)}) copy-start(f32[2,2,64]{2,1,0:T(2,128)} %copy-done.18) | copy-start | bytes 3076
  (3 other events, 2.8 us)
Sparse Core Ops, SparseCore 0:
  35.6 84.0 all-gather.14
  122.4 79.7 all-gather.12
  205.0 79.8 all-gather.8
  287.5 79.7 all-gather.10
  417.1 81.1 reduce-scatter.1
where the time goes:
time: 508 us; the launch traced here: 506 us
  waiting for transfers between devices  346 us (68%)
  matrix products  115 us (23%)
  between operations  14.6 us (3%)
  blocking collectives  12.6 us (2%)
  local copies, waits for them, and re-layouts  12 us (2%)
    all_gather x4, waiting for transfers between devices, prefix(): gathered = jax.tree.map(lambda a: lax.all_gather(a, axis), part)  267 us
    dot_general x63, matrix products, compose(): jnp.einsum('hij,hjk->hik', late_map, early_shift, precision=highest)  78.3 us
    reduce_scatter x1, waiting for transfers between devices, body(): lax.psum_scatter(partial_out, 'head', scatter_dimension=1, tiled=True)  77.4 us
    all_gather x1, blocking collectives, body(): lax.all_gather(out_grad, 'head', axis=1, tiled=True)  12.6 us
  transfers between devices with their start and end apart: 5, of which 5 were waited for; matrix products, arithmetic and copies ran while one was open for 13% of the time, Pallas kernels for 0%

commit v1 on v0

--- a/solution.py
+++ b/solution.py
@@ -1,3 +1,4 @@
+import functools
 import jax
 import jax.numpy as jnp
 from jax import lax
@@ -6,6 +7,18 @@
 BLOCK = 64
 epsilon = 1e-06
 highest = lax.Precision.HIGHEST
+
+
+def push_the_fields(m, lane_axis):
+    return jnp.concatenate(
+        jax.lax.all_to_all(
+            jnp.stack([m] * jax.lax.psum(1, axis_name=lane_axis), axis=0), lane_axis, 0, 0
+        ),
+        axis=1,
+    )
+
+
+_settle_trees = functools.partial(push_the_fields, lane_axis="head")
 
 
 def prefix(part, axis, combine, identity, reverse):
@@ -131,7 +144,7 @@
     offset = joined_state[..., head_width:]
     query_effect = joined_outputs[..., :head_width]
     attended_grad = lax.dot_general(
-        lax.all_gather(out_grad, "head", axis=1, tiled=True),
+        _settle_trees(out_grad),
         out_weight,
         (((1,), (1,)), ((), ())),
         preferred_element_type=jnp.float32,

time: 508 us -> 475 us (0.935)
  the two profiles are of different devices: /device:TPU:8 before, /device:TPU:2 now
where the time goes in v1:
time: 475 us; the launch traced here: 474 us
  waiting for transfers between devices  313 us (66%)
  matrix products  114 us (24%)
  between operations  14.5 us (3%)
  local copies, waits for them, and re-layouts  14.4 us (3%)
  blocking collectives  9.85 us (2%)
    all_gather x4, waiting for transfers between devices, prefix(): gathered = jax.tree.map(lambda a: lax.all_gather(a, axis), part)  313 us
    dot_general x63, matrix products, compose(): jnp.einsum('hij,hjk->hik', late_map, early_shift, precision=highest)  78.2 us
    all_to_all x1, blocking collectives, push_the_fields(): jax.lax.all_to_all(jnp.stack([m] * jax.lax.psum(1, axis_name=lane_axis),...  9.85 us
  transfers between devices with their start and end apart: 5, of which 4 were waited for; matrix products, arithmetic and copies ran while one was open for 25% of the time, Pallas kernels for 0%

profile of v1, /device:TPU:2, one launch (start us, length us, event | category | flops | bytes accessed | tf_op | source)
XLA Modules:
  0.0 473.6 jit_solution(9930602397456704419)
XLA Ops:
  16.8 3.9 while.78
  24.0 9.9 %all_to_all.5 = bf16[4,128,256]{2,1,0:T(8,128)(2,1)S(1)} all-to-all(bf16[4,128,256]{2,1,0:T(8,128)(2,1)S(1)} %stack.2), channel_id=1, replica_groups=mesh['seq'=64,'head'=4] {'head'}, dimensions={0} | all-to-all | bytes 524288 | tf_op jit(solution)/shard_map/all_to_all | solution.py:14
  34.6 1.9 convolution_bitcast_fusion.5
  37.2 70.4 %all-gather.9.cloned.1.call-done = f32[128,128,128]{2,1,0:T(8,128)} async-done(((f32[2,128,128]{2,1,0:T(8,128)}), f32[128,128,128]{2,1,0:T(8,128)}) %all-gather.9.cloned.1.call-update) | async-done | bytes 8388624 | tf_op jit(solution)/shard_map/all_gather | solution.py:28
  107.6 82.6 %all-gather.11.cloned.1.call-done = f32[128,128,128]{2,1,0:T(8,128)} async-done(((f32[2,128,128]{2,1,0:T(8,128)}), f32[128,128,128]{2,1,0:T(8,128)}) %all-gather.11.cloned.1.call-update) | async-done | bytes 8388624 | tf_op jit(solution)/shard_map/all_gather | solution.py:28
  190.3 3.5 while.80
  195.7 77.2 %all-gather.13.cloned.1.call-done = f32[128,128,128]{2,1,0:T(8,128)} async-done(((f32[2,128,128]{2,1,0:T(8,128)}), f32[128,128,128]{2,1,0:T(8,128)}) %all-gather.13.cloned.1.call-update) | async-done | bytes 8388624 | tf_op jit(solution)/shard_map/all_gather | solution.py:28
  273.0 82.4 %all-gather.15.cloned.1.call-done = f32[128,128,128]{2,1,0:T(8,128)} async-done(((f32[2,128,128]{2,1,0:T(8,128)}), f32[128,128,128]{2,1,0:T(8,128)}) %all-gather.15.cloned.1.call-update) | async-done | bytes 8388624 | tf_op jit(solution)/shard_map/all_gather | solution.py:28
  355.3 81.6 %while.81 = (s32[]{:T(128)}, f32[2,128,128]{2,1,0:T(8,128)S(1)}, s32[]{:T(128)}, f32[64,2,128,128]{3,2,1,0:T(8,128)}, f32[64,2,128,128]{3,2,1,0:T(8,128)}, /*index=5*/s32[]{:T(128)}, s32[]{:T(128)}, s32[]{:T(128)}, s32[]{:T(128)}) while((s32[]{:T(128)}, f32[2,128,128]{2,1,0:T(8,128)S(1)}, s32[]{:T(128)}, f32[64,2,128,128]{3,2,1,0:T(8,128)}, ...), condition=%wide.region_10.11_spmd, body=%wide.region_9.10_spmd.sunk | while | flops 50364420 | bytes 787595 | solution.py:37
  355.4 1.2 convolution_add_fusion.38
  356.7 1.2 convolution_add_fusion.38
  359.3 1.2 convolution_add_fusion.38
  360.6 1.2 convolution_add_fusion.38
  365.7 1.2 convolution_add_fusion.38
  369.6 1.2 convolution_add_fusion.38
  373.5 1.2 convolution_add_fusion.38
  376.1 1.2 convolution_add_fusion.38
  386.4 1.2 convolution_add_fusion.38
  401.9 1.2 convolution_add_fusion.38
  405.8 1.2 convolution_add_fusion.38
  421.3 1.2 convolution_add_fusion.38
  425.1 1.2 convolution_add_fusion.38
  439.6 10.3 %while.82 = (s32[]{:T(128)}, f32[2,128,128]{2,1,0:T(8,128)S(1)}, f32[2,2,64,128]{3,2,0,1:T(8,128)}, f32[2,2,64,128]{3,2,0,1:T(8,128)}, f32[2,2,64,128]{3,2,1,0:T...) while((s32[]{:T(128)}, f32[2,128,128]{2,1,0:T(8,128)S(1)}, ...), condition=%wide.region_12.13_spmd, body=%wide.region_11.12_spmd.sunk | while | flops 176275456 | bytes 2367137 | solution.py:97
  465.5 1.5 convert_element_type.51
  (289 shorter events, 114.1 us)
Async XLA Ops:
  7.2 27.1 %copy-start = (bf16[256,1024]{1,0:T(8,128)(2,1)S(1)}, bf16[256,1024]{1,0:T(8,128)(2,1)}, u32[]{:S(2)}) copy-start(bf16[256,1024]{1,0:T(8,128)(2,1)} %param.20) | copy-start | bytes 1572868
  7.2 100.5 %all-gather.9.cloned.1.call-start = ((), (), s32[]{:S(2)}) async-start(), calls=%async_computation.3 | async-start | bytes 8519680 | tf_op jit(solution)/shard_map/all_gather | solution.py:28
  7.2 4.0 copy-start.8
  8.4 8.4 %copy-start.15 = (f32[2,2,64]{2,1,0:T(2,128)}, f32[2,2,64]{2,1,0:T(2,128)S(1)}, u32[]{:S(2)}) copy-start(f32[2,2,64]{2,1,0:T(2,128)S(1)} %fusion.97) | copy-start | bytes 3076
  9.4 7.4 %copy-start.14 = (f32[2,2,64]{2,1,0:T(2,128)}, f32[2,2,64]{2,1,0:T(2,128)S(1)}, u32[]{:S(2)}) copy-start(f32[2,2,64]{2,1,0:T(2,128)S(1)} %fusion.96) | copy-start | bytes 3076
  10.3 0.8 copy-start.10
  10.3 5.4 %copy-start.12 = (f32[2,2,64]{2,1,0:T(2,128)}, f32[2,2,64]{2,1,0:T(2,128)S(1)}, u32[]{:S(2)}) copy-start(f32[2,2,64]{2,1,0:T(2,128)S(1)} %get-tuple-element.713) | copy-start | bytes 3076
  11.6 0.6 copy-start.1
  15.0 0.6 copy-start.7
  21.5 168.7 %all-gather.11.cloned.1.call-start = ((), (), s32[]{:S(2)}) async-start(), calls=%async_computation.4 | async-start | bytes 8519680 | tf_op jit(solution)/shard_map/all_gather | solution.py:28
  22.3 250.7 %all-gather.13.cloned.1.call-start = ((), (), s32[]{:S(2)}) async-start(), calls=%async_computation.5 | async-start | bytes 8519680 | tf_op jit(solution)/shard_map/all_gather | solution.py:28
  23.1 332.2 %all-gather.15.cloned.1.call-start = ((), (), s32[]{:S(2)}) async-start(), calls=%async_computation.6 | async-start | bytes 8519680 | tf_op jit(solution)/shard_map/all_gather | solution.py:28
  36.5 429.0 %reduce-scatter.2.cloned.1.call-start = ((), (), s32[]{:S(2)}) async-start(), calls=%async_computation.2 | async-start | bytes 655360 | tf_op jit(solution)/shard_map/reduce_scatter | solution.py:175
  439.6 17.2 %copy-start.2 = (f32[2,2,64,64]{3,2,1,0:T(8,128)S(1)}, f32[2,2,64,64]{3,2,1,0:T(8,128)}, u32[]{:S(2)}) copy-start(f32[2,2,64,64]{3,2,1,0:T(8,128)} %copy-done.1) | copy-start | bytes 196612
  449.9 8.0 %copy-start.9 = (f32[64,64]{1,0:T(8,128)S(1)}, f32[64,64]{1,0:T(8,128)}, u32[]{:S(2)}) copy-start(f32[64,64]{1,0:T(8,128)} %copy-done.8) | copy-start | bytes 49156
  449.9 9.2 %copy-start.11 = (pred[64,64]{1,0:T(8,128)(4,1)S(1)}, pred[64,64]{1,0:T(8,128)(4,1)}, u32[]{:S(2)}) copy-start(pred[64,64]{1,0:T(8,128)(4,1)} %copy-done.10) | copy-start | bytes 12292
  449.9 10.0 %copy-start.5 = (f32[2,2,64,64]{3,2,1,0:T(8,128)S(1)}, f32[2,2,64,64]{3,2,1,0:T(8,128)}, u32[]{:S(2)}) copy-start(f32[2,2,64,64]{3,2,1,0:T(8,128)} %get-tuple-element.516) | copy-start | bytes 196612
  449.9 10.0 %copy-start.13 = (f32[2,2,64]{2,1,0:T(2,128)S(1)}, f32[2,2,64]{2,1,0:T(2,128)}, u32[]{:S(2)}) copy-start(f32[2,2,64]{2,1,0:T(2,128)} %copy-done.12) | copy-start | bytes 3076
  449.9 10.5 %copy-start.4 = (f32[2,2,64,128]{3,2,0,1:T(8,128)S(1)}, f32[2,2,64,128]{3,2,0,1:T(8,128)}, u32[]{:S(2)}) copy-start(f32[2,2,64,128]{3,2,0,1:T(8,128)} %get-tuple-element.517) | copy-start | bytes 393220
  449.9 11.0 %copy-start.16 = (f32[2,2,64]{2,1,0:T(2,128)S(1)}, f32[2,2,64]{2,1,0:T(2,128)}, u32[]{:S(2)}) copy-start(f32[2,2,64]{2,1,0:T(2,128)} %copy-done.15) | copy-start | bytes 3076
  449.9 12.5 %copy-start.6 = (f32[2,2,64,128]{3,2,1,0:T(8,128)S(1)}, f32[2,2,64,128]{3,2,1,0:T(8,128)}, u32[]{:S(2)}) copy-start(f32[2,2,64,128]{3,2,1,0:T(8,128)} %get-tuple-element.519) | copy-start | bytes 393220
  450.0 13.6 %copy-start.3 = (f32[2,2,64,128]{3,2,0,1:T(8,128)S(1)}, f32[2,2,64,128]{3,2,0,1:T(8,128)}, u32[]{:S(2)}) copy-start(f32[2,2,64,128]{3,2,0,1:T(8,128)} %get-tuple-element.515) | copy-start | bytes 393220
Sparse Core Ops, SparseCore 0:
  21.7 85.9 all-gather.8
  110.4 79.7 all-gather.10
  193.0 79.9 all-gather.12
  275.6 79.6 all-gather.14
  357.7 18.8 reduce-scatter.1
